TPU v7x, 512 devices: a whole 4x4x16 slice. The times are simulated.
512 devices in a mesh: tile: 128 (over z, y_hi, x), lev: 4 (over y_lo, core).
Axes of the slice: x: 4, y: 4 (y_hi: 2, y_lo: 2; y = y_hi * 2 + y_lo), z: 16, core: 2. Of those that a mesh axis runs over, the one named last changes fastest.
Arguments:
- forcing: float32 [2, 52, 6144, 128], P(None, 'lev', 'tile'), may hold values from -6 to 6
- lateral_mix: float32 [52], P('lev'), may hold values from 0.05 to 0.15
- sea_mask: int32 [6144, 128], P('tile'), may hold values 0 or 1
- convective: int32 [6144, 128], P('tile'), may hold values 0 or 1
- mixing_inverse: float32 [2, 2, 52, 52], replicated, may hold values from -1.5 to 1.5
- seam_links: int32 [128, 8], P('tile'), may hold values from 0 to 511, as said below
Outputs:
- swept: float32 [2, 52, 6144, 128], P(None, 'lev', 'tile')
Inputs may be any that keep to these rules, and one draw needn't show every extreme that they name: Tile t sits at row t // 16 and column t % (16) of a grid of 8 rows that closes in both directions. seam_links[t, k] = 4 * s + code, where s is the tile beside t in that grid toward the previous row (k = 0), the next row (k = 1), the previous column (k = 2), the next column (k = 3), and diagonally (k = 4: previous row and column, 5: previous row and next column, 6: next row and previous column, 7: next row and next column).
All inputs are finite; a program needn't handle non-finite values. No bound on the sum of `sea_mask` or of `convective` on one device may be relied on, other than what follows from the above.
Results may differ from a plain program's by a relative error of at most 0.0001.
Values sent between devices are 32-bit elements; how exact they have to be, the bound alone decides.
No kernel may reach another device: no remote copies, remote signals or barrier semaphores. Data moves between devices by JAX's collectives and lax.ppermute only.
A program may use at most 64 MiB of HBM per device.

v0:
```python
import jax
import jax.numpy as jnp
from jax import lax
from jax.sharding import PartitionSpec as P

STEPS = 2
SLOT_STEPS = ((-1, 0), (1, 0), (0, -1), (0, 1), (-1, -1), (-1, 1), (1, -1), (1, 1))


def passed_along(value, axis, steps):
    count = lax.axis_size(axis)
    pairs = [(source, (source + steps) % count) for source in range(count)]
    return lax.ppermute(value, axis, pairs)


def strip_set(field):
    return jnp.concatenate(
        [
            field[..., 0, :],
            field[..., -1, :],
            field[..., :, 0],
            field[..., :, -1],
            field[..., 0, 0:1],
            field[..., 0, -1:],
            field[..., -1, 0:1],
            field[..., -1, -1:],
        ],
        axis=-1,
    )


def assemble(field, south, north, west, east, corners):
    middle = jnp.concatenate([west[..., None], field, east[..., None]], axis=-1)
    top_row = jnp.concatenate([corners[0][..., None], south, corners[1][..., None]], axis=-1)
    bottom_row = jnp.concatenate([corners[2][..., None], north, corners[3][..., None]], axis=-1)
    return jnp.concatenate([top_row[..., None, :], middle, bottom_row[..., None, :]], axis=-2)


def stencil(extended, field, rate, wet):
    edge_sum = (
        extended[..., :-2, 1:-1]
        + extended[..., 2:, 1:-1]
        + extended[..., 1:-1, :-2]
        + extended[..., 1:-1, 2:]
    )
    diag_sum = (
        extended[..., :-2, :-2]
        + extended[..., :-2, 2:]
        + extended[..., 2:, :-2]
        + extended[..., 2:, 2:]
    )
    return wet * ((1.0 - 6.0 * rate) * field + rate * edge_sum + 0.5 * rate * diag_sum)


def offset_slots(width, count):
    listing = {}
    for column in range(width):
        for slot in range(8):
            row_move, col_move = SLOT_STEPS[slot]
            moved_by = row_move * width + (column + col_move) % width - column
            distance = -moved_by % count
            if distance not in listing:
                listing[distance] = []
            listing[distance].append(slot)
    return listing


def seam_select(own_strips, seam_links):
    tile_count = lax.axis_size("tile")
    listing = offset_slots(tile_count // 8, tile_count)
    offsets = sorted(listing)
    received = []
    for shift_by in offsets:
        filled = passed_along(own_strips, "tile", shift_by)
        received.append(filled)
    stacked = jnp.stack(received)
    tile_here = lax.axis_index("tile")
    source = seam_links[0] // 4
    codes = seam_links[0] % 4
    distance = (tile_here - source) % tile_count
    offset_table = jnp.array(offsets, jnp.int32)
    selector = (distance[:, None] == offset_table[None, :]).astype(jnp.float32)
    chosen = jnp.einsum("sk,ktlp->stlp", selector, stacked, precision=lax.Precision.HIGHEST)
    return (chosen, codes)


def level_horizontal(adjoint, lateral_mix, wet, seam_links):
    rows = adjoint.shape[2]
    cols = adjoint.shape[3]
    chosen, codes = seam_select(strip_set(adjoint), seam_links)

    def edge(slot, first, last, length):
        part_a = chosen[slot][:, :, first : first + length]
        part_b = chosen[slot][:, :, last : last + length]
        strip = jnp.where(codes[slot] % 2 == 0, part_a, part_b)
        return jnp.where(codes[slot] // 2 == 1, strip[..., ::-1], strip)

    base = 2 * cols + 2 * rows

    def corner(slot):
        return lax.dynamic_index_in_dim(chosen[slot], base + codes[slot], axis=2, keepdims=False)

    south = edge(0, 0, cols, cols)
    north = edge(1, 0, cols, cols)
    west = edge(2, 2 * cols, 2 * cols + rows, rows)
    east = edge(3, 2 * cols, 2 * cols + rows, rows)
    corners = [corner(4), corner(5), corner(6), corner(7)]
    extended = assemble(adjoint, south, north, west, east, corners)
    rate = lateral_mix[None, :, None, None]
    return stencil(extended, adjoint, rate, wet[None, None])


def local(forcing, lateral_mix, sea_mask, convective, mixing_inverse, seam_links):
    wet = sea_mask.astype(jnp.float32)
    depth = forcing.shape[1]
    lev_here = lax.axis_index("lev")
    adjoint = forcing
    for step in range(STEPS):
        lateral = level_horizontal(adjoint, lateral_mix, wet, seam_links)
        own_levels = lax.dynamic_slice_in_dim(mixing_inverse, lev_here * depth, depth, axis=3)
        both_states = jnp.einsum(
            "tsml,tmxy->tslxy",
            own_levels,
            lax.all_gather(lateral, "lev", axis=1, tiled=True),
            precision=lax.Precision.HIGHEST,
        )
        adjoint = jnp.where(convective[None, None] == 1, both_states[:, 1], both_states[:, 0])
    return adjoint


def solution(mesh):
    return jax.shard_map(
        local,
        mesh=mesh,
        in_specs=(
            P(None, "lev", "tile", None),
            P("lev"),
            P("tile", None),
            P("tile", None),
            P(),
            P("tile", None),
        ),
        out_specs=P(None, "lev", "tile", None),
        check_vma=False,
    )
```

profile of v0, /device:TPU:1, one launch (start us, length us, event | category | flops | bytes accessed | tf_op | source)
XLA Modules:
  0.0 261.6 jit_solution(10945361443010133119)
XLA Ops:
  6.5 1.0 fusion.37
  7.5 1.4 slice_reduce_fusion
  8.9 1.6 fusion.36
  11.0 0.3 copy.871
  11.3 0.3 copy.872
  11.8 3.9 %collective-permute-start = (f32[2,13,356]{2,0,1:T(2,128)S(1)}, f32[2,13,356]{2,0,1:T(2,128)S(1)}, u32[]{:S(2)}, u32[]{:S(2)}) collective-permute-start(f32[2,13,356]{2,0,1:T(2,128)S(1)} %concatenate.58), channel_id=1, source_target_pairs={{0,4},{4,8},{8,12},{12,16},{16,20},{20,24},{24,28},{28,32},{32,36}... | collective-permute-start | bytes 111080 | tf_op jit(solution)/shard_map/ppermute | solution.py:13
  15.7 8.5 %collective-permute-start.1 = (f32[2,13,356]{2,0,1:T(2,128)S(1)}, f32[2,13,356]{2,0,1:T(2,128)S(1)}, u32[]{:S(2)}, u32[]{:S(2)}) collective-permute-start(f32[2,13,356]{2,0,1:T(2,128)S(1)} %concatenate.58), channel_id=1, source_target_pairs={{0,60},{4,64},{8,68},{12,72},{16,76},{20,80},{24,84},{28,88},{32,9... | collective-permute-start | bytes 111080 | tf_op jit(solution)/shard_map/ppermute | solution.py:13
  24.2 6.1 %collective-permute-start.2 = (f32[2,13,356]{2,0,1:T(2,128)S(1)}, f32[2,13,356]{2,0,1:T(2,128)S(1)}, u32[]{:S(2)}, u32[]{:S(2)}) collective-permute-start(f32[2,13,356]{2,0,1:T(2,128)S(1)} %concatenate.58), channel_id=1, source_target_pairs={{0,64},{4,68},{8,72},{12,76},{16,80},{20,84},{24,88},{28,92},{32,9... | collective-permute-start | bytes 111080 | tf_op jit(solution)/shard_map/ppermute | solution.py:13
  30.4 2.2 collective-permute-start.3
  32.6 14.2 %collective-permute-start.4 = (f32[2,13,356]{2,0,1:T(2,128)S(1)}, f32[2,13,356]{2,0,1:T(2,128)S(1)}, u32[]{:S(2)}, u32[]{:S(2)}) collective-permute-start(f32[2,13,356]{2,0,1:T(2,128)S(1)} %concatenate.58), channel_id=1, source_target_pairs={{0,124},{4,128},{8,132},{12,136},{16,140},{20,144},{24,148},{28,15... | collective-permute-start | bytes 111080 | tf_op jit(solution)/shard_map/ppermute | solution.py:13
  46.9 1.9 collective-permute-start.5
  48.8 7.3 %collective-permute-start.6 = (f32[2,13,356]{2,0,1:T(2,128)S(1)}, f32[2,13,356]{2,0,1:T(2,128)S(1)}, u32[]{:S(2)}, u32[]{:S(2)}) collective-permute-start(f32[2,13,356]{2,0,1:T(2,128)S(1)} %concatenate.58), channel_id=1, source_target_pairs={{0,444},{4,448},{8,452},{12,456},{16,460},{20,464},{24,468},{28,47... | collective-permute-start | bytes 111080 | tf_op jit(solution)/shard_map/ppermute | solution.py:13
  56.1 4.0 %collective-permute-start.7 = (f32[2,13,356]{2,0,1:T(2,128)S(1)}, f32[2,13,356]{2,0,1:T(2,128)S(1)}, u32[]{:S(2)}, u32[]{:S(2)}) collective-permute-start(f32[2,13,356]{2,0,1:T(2,128)S(1)} %concatenate.58), channel_id=1, source_target_pairs={{0,448},{4,452},{8,456},{12,460},{16,464},{20,468},{24,472},{28,47... | collective-permute-start | bytes 111080 | tf_op jit(solution)/shard_map/ppermute | solution.py:13
  60.1 1.9 collective-permute-start.8
  62.0 10.3 %collective-permute-start.9 = (f32[2,13,356]{2,0,1:T(2,128)S(1)}, f32[2,13,356]{2,0,1:T(2,128)S(1)}, u32[]{:S(2)}, u32[]{:S(2)}) collective-permute-start(f32[2,13,356]{2,0,1:T(2,128)S(1)} %concatenate.58), channel_id=1, source_target_pairs={{0,508},{4,0},{8,4},{12,8},{16,12},{20,16},{24,20},{28,24},{32,28}... | collective-permute-start | bytes 111080 | tf_op jit(solution)/shard_map/ppermute | solution.py:13
  72.3 0.7 fusion.42
  89.1 0.8 stack.76
  89.9 0.4 fusion.26
  91.5 0.4 copy.894
  92.3 0.4 copy.896
  92.9 1.3 maximum_maximum_fusion
  94.2 1.5 fusion.16
  95.8 1.0 copy.906
  97.4 38.6 %all-gather.3.cloned.1.call-done = f32[2,52,48,128]{3,2,0,1:T(8,128)} async-done(((f32[2,13,48,128]{3,2,0,1:T(8,128)}), f32[2,52,48,128]{3,2,0,1:T(8,128)}) %all-gather.3.cloned.1.call-update) | async-done | bytes 2555920 | tf_op jit(solution)/shard_map/all_gather | solution.py:124
  135.9 4.8 %fusion.2 = f32[2,2,13,48,128]{4,2,3,1,0:T(8,128)S(1)} fusion(f32[2,52,48,128,1]{3,2,0,1,4:T(8,128)} %bitcast.191, f32[2,2,52,13]{2,3,1,0:T(8,128)S(1)} %copy.953), kind=kOutput, calls=%fused_computation.2 | convolution fusion | flops 199360512 | bytes 3844672 | tf_op jit(solution)/shard_map/tsml,tmxy->tslxy/dot_general | solution.py:121
  140.9 0.3 fusion.35
  141.2 0.4 copy.910
  141.6 0.3 copy.911
  142.0 3.1 %collective-permute-start.10 = (f32[2,13,356]{2,1,0:T(8,128)S(1)}, f32[2,13,356]{2,1,0:T(8,128)S(1)}, u32[]{:S(2)}, u32[]{:S(2)}) collective-permute-start(f32[2,13,356]{2,1,0:T(8,128)S(1)} %concatenate.66), channel_id=1, source_target_pairs={{0,4},{4,8},{8,12},{12,16},{16,20},{20,24},{24,28},{28,32},{32,36}... | collective-permute-start | bytes 111080 | tf_op jit(solution)/shard_map/ppermute | solution.py:13
  145.1 7.8 %collective-permute-start.11 = (f32[2,13,356]{2,1,0:T(8,128)S(1)}, f32[2,13,356]{2,1,0:T(8,128)S(1)}, u32[]{:S(2)}, u32[]{:S(2)}) collective-permute-start(f32[2,13,356]{2,1,0:T(8,128)S(1)} %concatenate.66), channel_id=1, source_target_pairs={{0,60},{4,64},{8,68},{12,72},{16,76},{20,80},{24,84},{28,88},{32,9... | collective-permute-start | bytes 111080 | tf_op jit(solution)/shard_map/ppermute | solution.py:13
  152.9 5.4 %collective-permute-start.12 = (f32[2,13,356]{2,1,0:T(8,128)S(1)}, f32[2,13,356]{2,1,0:T(8,128)S(1)}, u32[]{:S(2)}, u32[]{:S(2)}) collective-permute-start(f32[2,13,356]{2,1,0:T(8,128)S(1)} %concatenate.66), channel_id=1, source_target_pairs={{0,64},{4,68},{8,72},{12,76},{16,80},{20,84},{24,88},{28,92},{32,9... | collective-permute-start | bytes 111080 | tf_op jit(solution)/shard_map/ppermute | solution.py:13
  158.3 1.9 collective-permute-start.13
  160.2 12.3 %collective-permute-start.14 = (f32[2,13,356]{2,1,0:T(8,128)S(1)}, f32[2,13,356]{2,1,0:T(8,128)S(1)}, u32[]{:S(2)}, u32[]{:S(2)}) collective-permute-start(f32[2,13,356]{2,1,0:T(8,128)S(1)} %concatenate.66), channel_id=1, source_target_pairs={{0,124},{4,128},{8,132},{12,136},{16,140},{20,144},{24,148},{28,15... | collective-permute-start | bytes 111080 | tf_op jit(solution)/shard_map/ppermute | solution.py:13
  172.6 1.9 collective-permute-start.15
  174.5 9.4 %collective-permute-start.16 = (f32[2,13,356]{2,1,0:T(8,128)S(1)}, f32[2,13,356]{2,1,0:T(8,128)S(1)}, u32[]{:S(2)}, u32[]{:S(2)}) collective-permute-start(f32[2,13,356]{2,1,0:T(8,128)S(1)} %concatenate.66), channel_id=1, source_target_pairs={{0,444},{4,448},{8,452},{12,456},{16,460},{20,464},{24,468},{28,47... | collective-permute-start | bytes 111080 | tf_op jit(solution)/shard_map/ppermute | solution.py:13
  184.0 1.9 collective-permute-start.17
  186.0 1.9 collective-permute-start.18
  187.9 8.1 %collective-permute-start.19 = (f32[2,13,356]{2,1,0:T(8,128)S(1)}, f32[2,13,356]{2,1,0:T(8,128)S(1)}, u32[]{:S(2)}, u32[]{:S(2)}) collective-permute-start(f32[2,13,356]{2,1,0:T(8,128)S(1)} %concatenate.66), channel_id=1, source_target_pairs={{0,508},{4,0},{8,4},{12,8},{16,12},{20,16},{24,20},{28,24},{32,28}... | collective-permute-start | bytes 111080 | tf_op jit(solution)/shard_map/ppermute | solution.py:13
  196.2 0.8 collective-permute-done.19
  197.0 0.6 fusion.21
  198.7 0.4 copy.924
  199.5 0.4 copy.925
  200.1 1.3 maximum_maximum_fusion.1
  201.4 1.5 fusion.8
  202.9 1.0 copy.933
  204.0 44.8 %all-gather.5.cloned.1.call-done = f32[2,52,48,128]{3,2,0,1:T(8,128)} async-done(((f32[2,13,48,128]{3,2,0,1:T(8,128)}), f32[2,52,48,128]{3,2,0,1:T(8,128)}) %all-gather.5.cloned.1.call-update) | async-done | bytes 2555920 | tf_op jit(solution)/shard_map/all_gather | solution.py:124
  248.8 4.8 %fusion = f32[2,2,13,48,128]{4,2,3,0,1:T(8,128)S(1)} fusion(f32[2,52,48,128]{3,2,0,1:T(8,128)} %all-gather.5.cloned.1.call-done, f32[2,2,52,13]{2,3,1,0:T(8,128)S(1)} %copy.953), kind=kOutput, calls=%fused_computation | convolution fusion | flops 199360512 | bytes 3844672 | tf_op jit(solution)/shard_map/tsml,tmxy->tslxy/dot_general | solution.py:121
  253.7 1.0 copy.937
  (133 shorter events, 5.5 us)
Async XLA Ops:
  6.5 90.5 %copy-start = (f32[2,2,52,52]{3,1,2,0:T(2,128)S(1)}, f32[2,2,52,52]{3,1,2,0:T(2,128)}, u32[]{:S(2)}) copy-start(f32[2,2,52,52]{3,1,2,0:T(2,128)} %param.12) | copy-start | bytes 129796
  6.5 129.4 %all-gather.3.cloned.1.call-start = ((), (), s32[]{:S(2)}) async-start(), calls=%async_computation | async-start | bytes 3194880 | tf_op jit(solution)/shard_map/all_gather | solution.py:124
  8.9 37.9 %copy-start.4 = (f32[13]{0:T(128)S(1)}, f32[13]{0:T(128)}, u32[]{:S(2)}) copy-start(f32[13]{0:T(128)} %param.9) | copy-start | bytes 160
  8.9 37.9 %copy-start.6 = (s32[1,8]{1,0:T(1,128)S(1)}, s32[1,8]{1,0:T(1,128)}, u32[]{:S(2)}) copy-start(s32[1,8]{1,0:T(1,128)} %param.13) | copy-start | bytes 100
  8.9 79.2 %copy-start.1 = (f32[2,13,48,128]{3,2,1,0:T(8,128)S(1)}, f32[2,13,48,128]{3,2,1,0:T(8,128)}, u32[]{:S(2)}) copy-start(f32[2,13,48,128]{3,2,1,0:T(8,128)} %param.8) | copy-start | bytes 1916932
  10.9 77.6 %copy-start.2 = (s32[48,128]{1,0:T(8,128)S(1)}, s32[48,128]{1,0:T(8,128)}, u32[]{:S(2)}) copy-start(s32[48,128]{1,0:T(8,128)} %param.10) | copy-start | bytes 73732
  11.8 35.1 %collective-permute-start = (f32[2,13,356]{2,0,1:T(2,128)S(1)}, f32[2,13,356]{2,0,1:T(2,128)S(1)}, u32[]{:S(2)}, u32[]{:S(2)}) collective-permute-start(f32[2,13,356]{2,0,1:T(2,128)S(1)} %concatenate.58), channel_id=1, source_target_pairs={{0,4},{4,8},{8,12},{12,16},{16,20},{20,24},{24,28},{28,32},{32,36}... | collective-permute-start | bytes 111080 | tf_op jit(solution)/shard_map/ppermute | solution.py:13
  15.7 33.1 %collective-permute-start.1 = (f32[2,13,356]{2,0,1:T(2,128)S(1)}, f32[2,13,356]{2,0,1:T(2,128)S(1)}, u32[]{:S(2)}, u32[]{:S(2)}) collective-permute-start(f32[2,13,356]{2,0,1:T(2,128)S(1)} %concatenate.58), channel_id=1, source_target_pairs={{0,60},{4,64},{8,68},{12,72},{16,76},{20,80},{24,84},{28,88},{32,9... | collective-permute-start | bytes 111080 | tf_op jit(solution)/shard_map/ppermute | solution.py:13
  24.2 31.8 %collective-permute-start.2 = (f32[2,13,356]{2,0,1:T(2,128)S(1)}, f32[2,13,356]{2,0,1:T(2,128)S(1)}, u32[]{:S(2)}, u32[]{:S(2)}) collective-permute-start(f32[2,13,356]{2,0,1:T(2,128)S(1)} %concatenate.58), channel_id=1, source_target_pairs={{0,64},{4,68},{8,72},{12,76},{16,80},{20,84},{24,88},{28,92},{32,9... | collective-permute-start | bytes 111080 | tf_op jit(solution)/shard_map/ppermute | solution.py:13
  30.4 29.7 %collective-permute-start.3 = (f32[2,13,356]{2,0,1:T(2,128)S(1)}, f32[2,13,356]{2,0,1:T(2,128)S(1)}, u32[]{:S(2)}, u32[]{:S(2)}) collective-permute-start(f32[2,13,356]{2,0,1:T(2,128)S(1)} %concatenate.58), channel_id=1, source_target_pairs={{0,68},{4,72},{8,76},{12,80},{16,84},{20,88},{24,92},{28,96},{32,1... | collective-permute-start | bytes 111080 | tf_op jit(solution)/shard_map/ppermute | solution.py:13
  32.6 29.4 %collective-permute-start.4 = (f32[2,13,356]{2,0,1:T(2,128)S(1)}, f32[2,13,356]{2,0,1:T(2,128)S(1)}, u32[]{:S(2)}, u32[]{:S(2)}) collective-permute-start(f32[2,13,356]{2,0,1:T(2,128)S(1)} %concatenate.58), channel_id=1, source_target_pairs={{0,124},{4,128},{8,132},{12,136},{16,140},{20,144},{24,148},{28,15... | collective-permute-start | bytes 111080 | tf_op jit(solution)/shard_map/ppermute | solution.py:13
  46.9 41.9 %collective-permute-start.5 = (f32[2,13,356]{2,0,1:T(2,128)S(1)}, f32[2,13,356]{2,0,1:T(2,128)S(1)}, u32[]{:S(2)}, u32[]{:S(2)}) collective-permute-start(f32[2,13,356]{2,0,1:T(2,128)S(1)} %concatenate.58), channel_id=1, source_target_pairs={{0,388},{4,392},{8,396},{12,400},{16,404},{20,408},{24,412},{28,41... | collective-permute-start | bytes 111080 | tf_op jit(solution)/shard_map/ppermute | solution.py:13
  48.8 40.0 %collective-permute-start.6 = (f32[2,13,356]{2,0,1:T(2,128)S(1)}, f32[2,13,356]{2,0,1:T(2,128)S(1)}, u32[]{:S(2)}, u32[]{:S(2)}) collective-permute-start(f32[2,13,356]{2,0,1:T(2,128)S(1)} %concatenate.58), channel_id=1, source_target_pairs={{0,444},{4,448},{8,452},{12,456},{16,460},{20,464},{24,468},{28,47... | collective-permute-start | bytes 111080 | tf_op jit(solution)/shard_map/ppermute | solution.py:13
  56.1 32.8 %collective-permute-start.7 = (f32[2,13,356]{2,0,1:T(2,128)S(1)}, f32[2,13,356]{2,0,1:T(2,128)S(1)}, u32[]{:S(2)}, u32[]{:S(2)}) collective-permute-start(f32[2,13,356]{2,0,1:T(2,128)S(1)} %concatenate.58), channel_id=1, source_target_pairs={{0,448},{4,452},{8,456},{12,460},{16,464},{20,468},{24,472},{28,47... | collective-permute-start | bytes 111080 | tf_op jit(solution)/shard_map/ppermute | solution.py:13
  60.1 28.9 %collective-permute-start.8 = (f32[2,13,356]{2,0,1:T(2,128)S(1)}, f32[2,13,356]{2,0,1:T(2,128)S(1)}, u32[]{:S(2)}, u32[]{:S(2)}) collective-permute-start(f32[2,13,356]{2,0,1:T(2,128)S(1)} %concatenate.58), channel_id=1, source_target_pairs={{0,452},{4,456},{8,460},{12,464},{16,468},{20,472},{24,476},{28,48... | collective-permute-start | bytes 111080 | tf_op jit(solution)/shard_map/ppermute | solution.py:13
  62.0 27.0 %collective-permute-start.9 = (f32[2,13,356]{2,0,1:T(2,128)S(1)}, f32[2,13,356]{2,0,1:T(2,128)S(1)}, u32[]{:S(2)}, u32[]{:S(2)}) collective-permute-start(f32[2,13,356]{2,0,1:T(2,128)S(1)} %concatenate.58), channel_id=1, source_target_pairs={{0,508},{4,0},{8,4},{12,8},{16,12},{20,16},{24,20},{28,24},{32,28}... | collective-permute-start | bytes 111080 | tf_op jit(solution)/shard_map/ppermute | solution.py:13
  88.1 1.8 copy-start.5
  95.7 1.6 copy-start.3
  96.8 152.0 %all-gather.5.cloned.1.call-start = ((), (), s32[]{:S(2)}) async-start(), calls=%async_computation.1 | async-start | bytes 3194880 | tf_op jit(solution)/shard_map/all_gather | solution.py:124
  142.0 30.6 %collective-permute-start.10 = (f32[2,13,356]{2,1,0:T(8,128)S(1)}, f32[2,13,356]{2,1,0:T(8,128)S(1)}, u32[]{:S(2)}, u32[]{:S(2)}) collective-permute-start(f32[2,13,356]{2,1,0:T(8,128)S(1)} %concatenate.66), channel_id=1, source_target_pairs={{0,4},{4,8},{8,12},{12,16},{16,20},{20,24},{24,28},{28,32},{32,36}... | collective-permute-start | bytes 111080 | tf_op jit(solution)/shard_map/ppermute | solution.py:13
  145.1 29.4 %collective-permute-start.11 = (f32[2,13,356]{2,1,0:T(8,128)S(1)}, f32[2,13,356]{2,1,0:T(8,128)S(1)}, u32[]{:S(2)}, u32[]{:S(2)}) collective-permute-start(f32[2,13,356]{2,1,0:T(8,128)S(1)} %concatenate.66), channel_id=1, source_target_pairs={{0,60},{4,64},{8,68},{12,72},{16,76},{20,80},{24,84},{28,88},{32,9... | collective-permute-start | bytes 111080 | tf_op jit(solution)/shard_map/ppermute | solution.py:13
  152.9 31.1 %collective-permute-start.12 = (f32[2,13,356]{2,1,0:T(8,128)S(1)}, f32[2,13,356]{2,1,0:T(8,128)S(1)}, u32[]{:S(2)}, u32[]{:S(2)}) collective-permute-start(f32[2,13,356]{2,1,0:T(8,128)S(1)} %concatenate.66), channel_id=1, source_target_pairs={{0,64},{4,68},{8,72},{12,76},{16,80},{20,84},{24,88},{28,92},{32,9... | collective-permute-start | bytes 111080 | tf_op jit(solution)/shard_map/ppermute | solution.py:13
  158.3 27.6 %collective-permute-start.13 = (f32[2,13,356]{2,1,0:T(8,128)S(1)}, f32[2,13,356]{2,1,0:T(8,128)S(1)}, u32[]{:S(2)}, u32[]{:S(2)}) collective-permute-start(f32[2,13,356]{2,1,0:T(8,128)S(1)} %concatenate.66), channel_id=1, source_target_pairs={{0,68},{4,72},{8,76},{12,80},{16,84},{20,88},{24,92},{28,96},{32,1... | collective-permute-start | bytes 111080 | tf_op jit(solution)/shard_map/ppermute | solution.py:13
  160.2 27.7 %collective-permute-start.14 = (f32[2,13,356]{2,1,0:T(8,128)S(1)}, f32[2,13,356]{2,1,0:T(8,128)S(1)}, u32[]{:S(2)}, u32[]{:S(2)}) collective-permute-start(f32[2,13,356]{2,1,0:T(8,128)S(1)} %concatenate.66), channel_id=1, source_target_pairs={{0,124},{4,128},{8,132},{12,136},{16,140},{20,144},{24,148},{28,15... | collective-permute-start | bytes 111080 | tf_op jit(solution)/shard_map/ppermute | solution.py:13
  172.6 23.5 %collective-permute-start.15 = (f32[2,13,356]{2,1,0:T(8,128)S(1)}, f32[2,13,356]{2,1,0:T(8,128)S(1)}, u32[]{:S(2)}, u32[]{:S(2)}) collective-permute-start(f32[2,13,356]{2,1,0:T(8,128)S(1)} %concatenate.66), channel_id=1, source_target_pairs={{0,388},{4,392},{8,396},{12,400},{16,404},{20,408},{24,412},{28,41... | collective-permute-start | bytes 111080 | tf_op jit(solution)/shard_map/ppermute | solution.py:13
  174.5 21.5 %collective-permute-start.16 = (f32[2,13,356]{2,1,0:T(8,128)S(1)}, f32[2,13,356]{2,1,0:T(8,128)S(1)}, u32[]{:S(2)}, u32[]{:S(2)}) collective-permute-start(f32[2,13,356]{2,1,0:T(8,128)S(1)} %concatenate.66), channel_id=1, source_target_pairs={{0,444},{4,448},{8,452},{12,456},{16,460},{20,464},{24,468},{28,47... | collective-permute-start | bytes 111080 | tf_op jit(solution)/shard_map/ppermute | solution.py:13
  184.0 12.1 %collective-permute-start.17 = (f32[2,13,356]{2,1,0:T(8,128)S(1)}, f32[2,13,356]{2,1,0:T(8,128)S(1)}, u32[]{:S(2)}, u32[]{:S(2)}) collective-permute-start(f32[2,13,356]{2,1,0:T(8,128)S(1)} %concatenate.66), channel_id=1, source_target_pairs={{0,448},{4,452},{8,456},{12,460},{16,464},{20,468},{24,472},{28,47... | collective-permute-start | bytes 111080 | tf_op jit(solution)/shard_map/ppermute | solution.py:13
  186.0 10.2 %collective-permute-start.18 = (f32[2,13,356]{2,1,0:T(8,128)S(1)}, f32[2,13,356]{2,1,0:T(8,128)S(1)}, u32[]{:S(2)}, u32[]{:S(2)}) collective-permute-start(f32[2,13,356]{2,1,0:T(8,128)S(1)} %concatenate.66), channel_id=1, source_target_pairs={{0,452},{4,456},{8,460},{12,464},{16,468},{20,472},{24,476},{28,48... | collective-permute-start | bytes 111080 | tf_op jit(solution)/shard_map/ppermute | solution.py:13
  187.9 9.1 %collective-permute-start.19 = (f32[2,13,356]{2,1,0:T(8,128)S(1)}, f32[2,13,356]{2,1,0:T(8,128)S(1)}, u32[]{:S(2)}, u32[]{:S(2)}) collective-permute-start(f32[2,13,356]{2,1,0:T(8,128)S(1)} %concatenate.66), channel_id=1, source_target_pairs={{0,508},{4,0},{8,4},{12,8},{16,12},{20,16},{24,20},{28,24},{32,28}... | collective-permute-start | bytes 111080 | tf_op jit(solution)/shard_map/ppermute | solution.py:13
Sparse Core Ops, SparseCore 0:
  96.9 38.9 all-gather.2
  204.1 44.6 all-gather.4
where the time goes:
time: 263 us; the launch traced here: 262 us
  starting transfers between devices  114 us (43%)
  waiting for transfers between devices  84.3 us (32%)
  between operations  29.8 us (11%)
  local copies, waits for them, and re-layouts  15.7 us (6%)
  matrix products  10.5 us (4%)
  other arithmetic  6.93 us (3%)
    ppermute x20, starting transfers between devices, passed_along(): return lax.ppermute(value, axis, pairs)  114 us
    all_gather x2, waiting for transfers between devices, local(): lax.all_gather(lateral, 'lev', axis=1, tiled=True)  83.4 us
    dot_general x2, matrix products, local(): jnp.einsum('tsml,tmxy->tslxy', own_levels, lax.all_gather(lateral, 'lev',...  9.63 us
  transfers between devices with their start and end apart: 22, of which 3 were waited for; matrix products, arithmetic and copies ran while one was open for 1% of the time, Pallas kernels for 0%

commit v1 on v0

--- a/solution.py
+++ b/solution.py
@@ -121,7 +121,9 @@
         both_states = jnp.einsum(
             "tsml,tmxy->tslxy",
             own_levels,
-            lax.all_gather(lateral, "lev", axis=1, tiled=True),
+            jnp.concatenate(
+                lax.all_to_all(jnp.stack([lateral] * lax.axis_size("lev")), "lev", 0, 0), axis=1
+            ),
             precision=lax.Precision.HIGHEST,
         )
         adjoint = jnp.where(convective[None, None] == 1, both_states[:, 1], both_states[:, 0])

time: 263 us -> 235 us (0.89)
  waiting for transfers between devices: 84.3 us -> 30.5 us
  blocking collectives: 0 us -> 36.6 us
  between operations: 29.8 us -> 16.1 us
  starting transfers between devices: 114 us -> 120 us
  matrix products: 10.5 us -> 5.76 us
    all_gather x2 -> x0, waiting for transfers between devices: 83.4 us -> none  [local(): lax.all_gather(lateral, 'lev', axis=1, tiled=True)]
    all_to_all x0 -> x1, blocking collectives: none -> 36.6 us  [local(): lax.all_to_all(jnp.stack([lateral] * lax.axis_size('lev')), 'lev', 0, 0)]
    all_to_all x0 -> x1, waiting for transfers between devices: none -> 29.4 us  [local(): lax.all_to_all(jnp.stack([lateral] * lax.axis_size('lev')), 'lev', 0, 0)]
    all_to_all x0 -> x1, starting transfers between devices: none -> 6.94 us  [local(): lax.all_to_all(jnp.stack([lateral] * lax.axis_size('lev')), 'lev', 0, 0)]
    dot_general x2, matrix products: 9.63 us -> 4.83 us  [local(): jnp.einsum('tsml,tmxy->tslxy', own_levels, jnp.concatenate(lax.all_to_all...]
  transfers between devices with their start and end apart: 22 -> 21, of which waited for: 3 -> 2; matrix products, arithmetic and copies ran while one was open for 1% -> 1% of each run, Pallas kernels for 0% -> 0%
where the time goes in v1:
time: 235 us; the launch traced here: 232 us
  starting transfers between devices  120 us (51%)
  blocking collectives  36.6 us (16%)
  waiting for transfers between devices  30.5 us (13%)
  local copies, waits for them, and re-layouts  16.3 us (7%)
  between operations  16.1 us (7%)
  other arithmetic  6.93 us (3%)
  matrix products  5.76 us (2%)
    ppermute x20, starting transfers between devices, passed_along(): return lax.ppermute(value, axis, pairs)  113 us
    all_to_all x1, blocking collectives, local(): lax.all_to_all(jnp.stack([lateral] * lax.axis_size('lev')), 'lev', 0, 0)  36.6 us
    all_to_all x1, waiting for transfers between devices, local(): lax.all_to_all(jnp.stack([lateral] * lax.axis_size('lev')), 'lev', 0, 0)  29.4 us
    all_to_all x1, starting transfers between devices, local(): lax.all_to_all(jnp.stack([lateral] * lax.axis_size('lev')), 'lev', 0, 0)  6.94 us
    dot_general x2, matrix products, local(): jnp.einsum('tsml,tmxy->tslxy', own_levels, jnp.concatenate(lax.all_to_all...  4.83 us
  transfers between devices with their start and end apart: 21, of which 2 were waited for; matrix products, arithmetic and copies ran while one was open for 1% of the time, Pallas kernels for 0%

profile of v1, /device:TPU:1, one launch (start us, length us, event | category | flops | bytes accessed | tf_op | source)
XLA Modules:
  0.0 232.2 jit_solution(13351951830591135667)
XLA Ops:
  0.0 1.0 fusion.37
  1.0 1.4 slice_reduce_fusion
  2.4 1.6 fusion.36
  4.4 0.3 copy.903
  4.7 0.3 copy.904
  5.3 3.9 %collective-permute-start = (f32[2,13,356]{2,0,1:T(2,128)S(1)}, f32[2,13,356]{2,0,1:T(2,128)S(1)}, u32[]{:S(2)}, u32[]{:S(2)}) collective-permute-start(f32[2,13,356]{2,0,1:T(2,128)S(1)} %concatenate.58), channel_id=1, source_target_pairs={{0,4},{4,8},{8,12},{12,16},{16,20},{20,24},{24,28},{28,32},{32,36}... | collective-permute-start | bytes 111080 | tf_op jit(solution)/shard_map/ppermute | solution.py:13
  9.2 8.5 %collective-permute-start.1 = (f32[2,13,356]{2,0,1:T(2,128)S(1)}, f32[2,13,356]{2,0,1:T(2,128)S(1)}, u32[]{:S(2)}, u32[]{:S(2)}) collective-permute-start(f32[2,13,356]{2,0,1:T(2,128)S(1)} %concatenate.58), channel_id=1, source_target_pairs={{0,60},{4,64},{8,68},{12,72},{16,76},{20,80},{24,84},{28,88},{32,9... | collective-permute-start | bytes 111080 | tf_op jit(solution)/shard_map/ppermute | solution.py:13
  17.7 6.1 %collective-permute-start.2 = (f32[2,13,356]{2,0,1:T(2,128)S(1)}, f32[2,13,356]{2,0,1:T(2,128)S(1)}, u32[]{:S(2)}, u32[]{:S(2)}) collective-permute-start(f32[2,13,356]{2,0,1:T(2,128)S(1)} %concatenate.58), channel_id=1, source_target_pairs={{0,64},{4,68},{8,72},{12,76},{16,80},{20,84},{24,88},{28,92},{32,9... | collective-permute-start | bytes 111080 | tf_op jit(solution)/shard_map/ppermute | solution.py:13
  23.8 2.2 collective-permute-start.3
  26.0 14.2 %collective-permute-start.4 = (f32[2,13,356]{2,0,1:T(2,128)S(1)}, f32[2,13,356]{2,0,1:T(2,128)S(1)}, u32[]{:S(2)}, u32[]{:S(2)}) collective-permute-start(f32[2,13,356]{2,0,1:T(2,128)S(1)} %concatenate.58), channel_id=1, source_target_pairs={{0,124},{4,128},{8,132},{12,136},{16,140},{20,144},{24,148},{28,15... | collective-permute-start | bytes 111080 | tf_op jit(solution)/shard_map/ppermute | solution.py:13
  40.3 1.9 collective-permute-start.5
  42.3 7.3 %collective-permute-start.6 = (f32[2,13,356]{2,0,1:T(2,128)S(1)}, f32[2,13,356]{2,0,1:T(2,128)S(1)}, u32[]{:S(2)}, u32[]{:S(2)}) collective-permute-start(f32[2,13,356]{2,0,1:T(2,128)S(1)} %concatenate.58), channel_id=1, source_target_pairs={{0,444},{4,448},{8,452},{12,456},{16,460},{20,464},{24,468},{28,47... | collective-permute-start | bytes 111080 | tf_op jit(solution)/shard_map/ppermute | solution.py:13
  49.6 4.0 %collective-permute-start.7 = (f32[2,13,356]{2,0,1:T(2,128)S(1)}, f32[2,13,356]{2,0,1:T(2,128)S(1)}, u32[]{:S(2)}, u32[]{:S(2)}) collective-permute-start(f32[2,13,356]{2,0,1:T(2,128)S(1)} %concatenate.58), channel_id=1, source_target_pairs={{0,448},{4,452},{8,456},{12,460},{16,464},{20,468},{24,472},{28,47... | collective-permute-start | bytes 111080 | tf_op jit(solution)/shard_map/ppermute | solution.py:13
  53.5 1.9 collective-permute-start.8
  55.5 10.3 %collective-permute-start.9 = (f32[2,13,356]{2,0,1:T(2,128)S(1)}, f32[2,13,356]{2,0,1:T(2,128)S(1)}, u32[]{:S(2)}, u32[]{:S(2)}) collective-permute-start(f32[2,13,356]{2,0,1:T(2,128)S(1)} %concatenate.58), channel_id=1, source_target_pairs={{0,508},{4,0},{8,4},{12,8},{16,12},{20,16},{24,20},{28,24},{32,28}... | collective-permute-start | bytes 111080 | tf_op jit(solution)/shard_map/ppermute | solution.py:13
  65.7 0.7 fusion.42
  82.2 0.8 stack.90
  83.0 0.4 fusion.26
  84.6 0.4 copy.926
  85.4 0.4 copy.928
  86.0 1.3 maximum_maximum_fusion
  87.3 1.5 fusion.16
  89.1 1.7 stack.91
  90.8 6.9 %all-to-all-start = ((f32[4,2,13,48,128]{4,3,2,1,0:T(8,128)}), f32[4,2,13,48,128]{4,3,2,1,0:T(8,128)S(1)}, u32[]{:S(2)}, u32[]{:S(2)}) async-start(f32[4,2,13,48,128]{4,3,2,1,0:T(8,128)} %stack.91), calls=%async_computation | async-start | bytes 5111808 | tf_op jit(solution)/shard_map/all_to_all | solution.py:125
  98.1 29.4 %all-to-all-done = f32[4,2,13,48,128]{4,3,2,1,0:T(8,128)S(1)} async-done(((f32[4,2,13,48,128]{4,3,2,1,0:T(8,128)}), f32[4,2,13,48,128]{4,3,2,1,0:T(8,128)S(1)}, u32[]{:S(2)}, u32[]{:S(2)}) %all-to-all-start) | async-done | bytes 2555936 | tf_op jit(solution)/shard_map/all_to_all | solution.py:125
  127.7 2.4 %fusion.2 = f32[2,2,13,48,128]{4,2,3,1,0:T(8,128)S(1)} fusion(f32[2,52,48,128,1]{3,2,1,0,4:T(8,128)S(1)} %bitcast.199, f32[2,2,52,13]{2,3,1,0:T(8,128)S(1)} %copy.987), kind=kOutput, calls=%fused_computation.2 | convolution fusion | flops 199360512 | bytes 3844672 | tf_op jit(solution)/shard_map/tsml,tmxy->tslxy/dot_general | solution.py:121
  130.2 0.3 fusion.35
  130.6 0.4 copy.943
  130.9 0.3 copy.944
  131.4 1.9 collective-permute-start.10
  133.3 5.2 %collective-permute-start.11 = (f32[2,13,356]{2,1,0:T(8,128)S(1)}, f32[2,13,356]{2,1,0:T(8,128)S(1)}, u32[]{:S(2)}, u32[]{:S(2)}) collective-permute-start(f32[2,13,356]{2,1,0:T(8,128)S(1)} %concatenate.66), channel_id=1, source_target_pairs={{0,60},{4,64},{8,68},{12,72},{16,76},{20,80},{24,84},{28,88},{32,9... | collective-permute-start | bytes 111080 | tf_op jit(solution)/shard_map/ppermute | solution.py:13
  138.5 4.0 %collective-permute-start.12 = (f32[2,13,356]{2,1,0:T(8,128)S(1)}, f32[2,13,356]{2,1,0:T(8,128)S(1)}, u32[]{:S(2)}, u32[]{:S(2)}) collective-permute-start(f32[2,13,356]{2,1,0:T(8,128)S(1)} %concatenate.66), channel_id=1, source_target_pairs={{0,64},{4,68},{8,72},{12,76},{16,80},{20,84},{24,88},{28,92},{32,9... | collective-permute-start | bytes 111080 | tf_op jit(solution)/shard_map/ppermute | solution.py:13
  142.5 1.9 collective-permute-start.13
  144.5 13.5 %collective-permute-start.14 = (f32[2,13,356]{2,1,0:T(8,128)S(1)}, f32[2,13,356]{2,1,0:T(8,128)S(1)}, u32[]{:S(2)}, u32[]{:S(2)}) collective-permute-start(f32[2,13,356]{2,1,0:T(8,128)S(1)} %concatenate.66), channel_id=1, source_target_pairs={{0,124},{4,128},{8,132},{12,136},{16,140},{20,144},{24,148},{28,15... | collective-permute-start | bytes 111080 | tf_op jit(solution)/shard_map/ppermute | solution.py:13
  158.0 1.9 collective-permute-start.15
  160.0 8.4 %collective-permute-start.16 = (f32[2,13,356]{2,1,0:T(8,128)S(1)}, f32[2,13,356]{2,1,0:T(8,128)S(1)}, u32[]{:S(2)}, u32[]{:S(2)}) collective-permute-start(f32[2,13,356]{2,1,0:T(8,128)S(1)} %concatenate.66), channel_id=1, source_target_pairs={{0,444},{4,448},{8,452},{12,456},{16,460},{20,464},{24,468},{28,47... | collective-permute-start | bytes 111080 | tf_op jit(solution)/shard_map/ppermute | solution.py:13
  168.4 3.7 %collective-permute-start.17 = (f32[2,13,356]{2,1,0:T(8,128)S(1)}, f32[2,13,356]{2,1,0:T(8,128)S(1)}, u32[]{:S(2)}, u32[]{:S(2)}) collective-permute-start(f32[2,13,356]{2,1,0:T(8,128)S(1)} %concatenate.66), channel_id=1, source_target_pairs={{0,448},{4,452},{8,456},{12,460},{16,464},{20,468},{24,472},{28,47... | collective-permute-start | bytes 111080 | tf_op jit(solution)/shard_map/ppermute | solution.py:13
  172.1 1.9 collective-permute-start.18
  174.1 10.3 %collective-permute-start.19 = (f32[2,13,356]{2,1,0:T(8,128)S(1)}, f32[2,13,356]{2,1,0:T(8,128)S(1)}, u32[]{:S(2)}, u32[]{:S(2)}) collective-permute-start(f32[2,13,356]{2,1,0:T(8,128)S(1)} %concatenate.66), channel_id=1, source_target_pairs={{0,508},{4,0},{8,4},{12,8},{16,12},{20,16},{24,20},{28,24},{32,28}... | collective-permute-start | bytes 111080 | tf_op jit(solution)/shard_map/ppermute | solution.py:13
  184.5 1.0 collective-permute-done.19
  185.5 0.6 fusion.21
  187.3 0.4 copy.957
  188.0 0.4 copy.958
  188.6 1.3 maximum_maximum_fusion.1
  189.9 1.5 fusion.8
  191.9 36.6 %all_to_all.10 = f32[4,2,13,48,128]{4,3,2,1,0:T(8,128)S(1)} all-to-all(f32[4,2,13,48,128]{4,3,2,1,0:T(8,128)S(1)} %stack.103), channel_id=1, replica_groups=mesh['tile'=128,'lev'=4] {'lev'}, dimensions={0} | all-to-all | bytes 5111808 | tf_op jit(solution)/shard_map/all_to_all | solution.py:125
  228.7 2.4 %fusion = f32[2,2,13,48,128]{4,2,3,0,1:T(8,128)S(1)} fusion(f32[2,52,48,128]{3,2,1,0:T(8,128)S(1)} %bitcast.198, f32[2,2,52,13]{2,3,1,0:T(8,128)S(1)} %copy.987), kind=kOutput, calls=%fused_computation | convolution fusion | flops 199360512 | bytes 3844672 | tf_op jit(solution)/shard_map/tsml,tmxy->tslxy/dot_general | solution.py:121
  231.2 1.0 copy.971
  (134 shorter events, 6.2 us)
Async XLA Ops:
  0.0 97.7 %copy-start = (f32[2,2,52,52]{3,1,2,0:T(2,128)S(1)}, f32[2,2,52,52]{3,1,2,0:T(2,128)}, u32[]{:S(2)}) copy-start(f32[2,2,52,52]{3,1,2,0:T(2,128)} %param.12) | copy-start | bytes 129796
  2.4 37.9 %copy-start.4 = (f32[13]{0:T(128)S(1)}, f32[13]{0:T(128)}, u32[]{:S(2)}) copy-start(f32[13]{0:T(128)} %param.9) | copy-start | bytes 160
  2.4 37.9 %copy-start.6 = (s32[1,8]{1,0:T(1,128)S(1)}, s32[1,8]{1,0:T(1,128)}, u32[]{:S(2)}) copy-start(s32[1,8]{1,0:T(1,128)} %param.13) | copy-start | bytes 100
  2.4 78.8 %copy-start.1 = (f32[2,13,48,128]{3,2,1,0:T(8,128)S(1)}, f32[2,13,48,128]{3,2,1,0:T(8,128)}, u32[]{:S(2)}) copy-start(f32[2,13,48,128]{3,2,1,0:T(8,128)} %param.8) | copy-start | bytes 1916932
  4.3 77.3 %copy-start.2 = (s32[48,128]{1,0:T(8,128)S(1)}, s32[48,128]{1,0:T(8,128)}, u32[]{:S(2)}) copy-start(s32[48,128]{1,0:T(8,128)} %param.10) | copy-start | bytes 73732
  5.3 35.1 %collective-permute-start = (f32[2,13,356]{2,0,1:T(2,128)S(1)}, f32[2,13,356]{2,0,1:T(2,128)S(1)}, u32[]{:S(2)}, u32[]{:S(2)}) collective-permute-start(f32[2,13,356]{2,0,1:T(2,128)S(1)} %concatenate.58), channel_id=1, source_target_pairs={{0,4},{4,8},{8,12},{12,16},{16,20},{20,24},{24,28},{28,32},{32,36}... | collective-permute-start | bytes 111080 | tf_op jit(solution)/shard_map/ppermute | solution.py:13
  9.2 33.1 %collective-permute-start.1 = (f32[2,13,356]{2,0,1:T(2,128)S(1)}, f32[2,13,356]{2,0,1:T(2,128)S(1)}, u32[]{:S(2)}, u32[]{:S(2)}) collective-permute-start(f32[2,13,356]{2,0,1:T(2,128)S(1)} %concatenate.58), channel_id=1, source_target_pairs={{0,60},{4,64},{8,68},{12,72},{16,76},{20,80},{24,84},{28,88},{32,9... | collective-permute-start | bytes 111080 | tf_op jit(solution)/shard_map/ppermute | solution.py:13
  17.7 31.8 %collective-permute-start.2 = (f32[2,13,356]{2,0,1:T(2,128)S(1)}, f32[2,13,356]{2,0,1:T(2,128)S(1)}, u32[]{:S(2)}, u32[]{:S(2)}) collective-permute-start(f32[2,13,356]{2,0,1:T(2,128)S(1)} %concatenate.58), channel_id=1, source_target_pairs={{0,64},{4,68},{8,72},{12,76},{16,80},{20,84},{24,88},{28,92},{32,9... | collective-permute-start | bytes 111080 | tf_op jit(solution)/shard_map/ppermute | solution.py:13
  23.8 29.7 %collective-permute-start.3 = (f32[2,13,356]{2,0,1:T(2,128)S(1)}, f32[2,13,356]{2,0,1:T(2,128)S(1)}, u32[]{:S(2)}, u32[]{:S(2)}) collective-permute-start(f32[2,13,356]{2,0,1:T(2,128)S(1)} %concatenate.58), channel_id=1, source_target_pairs={{0,68},{4,72},{8,76},{12,80},{16,84},{20,88},{24,92},{28,96},{32,1... | collective-permute-start | bytes 111080 | tf_op jit(solution)/shard_map/ppermute | solution.py:13
  26.0 29.4 %collective-permute-start.4 = (f32[2,13,356]{2,0,1:T(2,128)S(1)}, f32[2,13,356]{2,0,1:T(2,128)S(1)}, u32[]{:S(2)}, u32[]{:S(2)}) collective-permute-start(f32[2,13,356]{2,0,1:T(2,128)S(1)} %concatenate.58), channel_id=1, source_target_pairs={{0,124},{4,128},{8,132},{12,136},{16,140},{20,144},{24,148},{28,15... | collective-permute-start | bytes 111080 | tf_op jit(solution)/shard_map/ppermute | solution.py:13
  40.3 41.6 %collective-permute-start.5 = (f32[2,13,356]{2,0,1:T(2,128)S(1)}, f32[2,13,356]{2,0,1:T(2,128)S(1)}, u32[]{:S(2)}, u32[]{:S(2)}) collective-permute-start(f32[2,13,356]{2,0,1:T(2,128)S(1)} %concatenate.58), channel_id=1, source_target_pairs={{0,388},{4,392},{8,396},{12,400},{16,404},{20,408},{24,412},{28,41... | collective-permute-start | bytes 111080 | tf_op jit(solution)/shard_map/ppermute | solution.py:13
  42.3 39.7 %collective-permute-start.6 = (f32[2,13,356]{2,0,1:T(2,128)S(1)}, f32[2,13,356]{2,0,1:T(2,128)S(1)}, u32[]{:S(2)}, u32[]{:S(2)}) collective-permute-start(f32[2,13,356]{2,0,1:T(2,128)S(1)} %concatenate.58), channel_id=1, source_target_pairs={{0,444},{4,448},{8,452},{12,456},{16,460},{20,464},{24,468},{28,47... | collective-permute-start | bytes 111080 | tf_op jit(solution)/shard_map/ppermute | solution.py:13
  49.6 32.5 %collective-permute-start.7 = (f32[2,13,356]{2,0,1:T(2,128)S(1)}, f32[2,13,356]{2,0,1:T(2,128)S(1)}, u32[]{:S(2)}, u32[]{:S(2)}) collective-permute-start(f32[2,13,356]{2,0,1:T(2,128)S(1)} %concatenate.58), channel_id=1, source_target_pairs={{0,448},{4,452},{8,456},{12,460},{16,464},{20,468},{24,472},{28,47... | collective-permute-start | bytes 111080 | tf_op jit(solution)/shard_map/ppermute | solution.py:13
  53.5 28.6 %collective-permute-start.8 = (f32[2,13,356]{2,0,1:T(2,128)S(1)}, f32[2,13,356]{2,0,1:T(2,128)S(1)}, u32[]{:S(2)}, u32[]{:S(2)}) collective-permute-start(f32[2,13,356]{2,0,1:T(2,128)S(1)} %concatenate.58), channel_id=1, source_target_pairs={{0,452},{4,456},{8,460},{12,464},{16,468},{20,472},{24,476},{28,48... | collective-permute-start | bytes 111080 | tf_op jit(solution)/shard_map/ppermute | solution.py:13
  55.5 26.7 %collective-permute-start.9 = (f32[2,13,356]{2,0,1:T(2,128)S(1)}, f32[2,13,356]{2,0,1:T(2,128)S(1)}, u32[]{:S(2)}, u32[]{:S(2)}) collective-permute-start(f32[2,13,356]{2,0,1:T(2,128)S(1)} %concatenate.58), channel_id=1, source_target_pairs={{0,508},{4,0},{8,4},{12,8},{16,12},{20,16},{24,20},{28,24},{32,28}... | collective-permute-start | bytes 111080 | tf_op jit(solution)/shard_map/ppermute | solution.py:13
  81.2 1.8 copy-start.5
  90.8 7.2 %copy-start.3 = (s32[48,128]{1,0:T(8,128)S(1)}, s32[48,128]{1,0:T(8,128)}, u32[]{:S(2)}) copy-start(s32[48,128]{1,0:T(8,128)} %param.11) | copy-start | bytes 73732
  90.8 36.7 %all-to-all-start = ((f32[4,2,13,48,128]{4,3,2,1,0:T(8,128)}), f32[4,2,13,48,128]{4,3,2,1,0:T(8,128)S(1)}, u32[]{:S(2)}, u32[]{:S(2)}) async-start(f32[4,2,13,48,128]{4,3,2,1,0:T(8,128)} %stack.91), calls=%async_computation | async-start | bytes 5111808 | tf_op jit(solution)/shard_map/all_to_all | solution.py:125
  131.4 26.6 %collective-permute-start.10 = (f32[2,13,356]{2,1,0:T(8,128)S(1)}, f32[2,13,356]{2,1,0:T(8,128)S(1)}, u32[]{:S(2)}, u32[]{:S(2)}) collective-permute-start(f32[2,13,356]{2,1,0:T(8,128)S(1)} %concatenate.66), channel_id=1, source_target_pairs={{0,4},{4,8},{8,12},{12,16},{16,20},{20,24},{24,28},{28,32},{32,36}... | collective-permute-start | bytes 111080 | tf_op jit(solution)/shard_map/ppermute | solution.py:13
  133.3 26.6 %collective-permute-start.11 = (f32[2,13,356]{2,1,0:T(8,128)S(1)}, f32[2,13,356]{2,1,0:T(8,128)S(1)}, u32[]{:S(2)}, u32[]{:S(2)}) collective-permute-start(f32[2,13,356]{2,1,0:T(8,128)S(1)} %concatenate.66), channel_id=1, source_target_pairs={{0,60},{4,64},{8,68},{12,72},{16,76},{20,80},{24,84},{28,88},{32,9... | collective-permute-start | bytes 111080 | tf_op jit(solution)/shard_map/ppermute | solution.py:13
  138.5 29.9 %collective-permute-start.12 = (f32[2,13,356]{2,1,0:T(8,128)S(1)}, f32[2,13,356]{2,1,0:T(8,128)S(1)}, u32[]{:S(2)}, u32[]{:S(2)}) collective-permute-start(f32[2,13,356]{2,1,0:T(8,128)S(1)} %concatenate.66), channel_id=1, source_target_pairs={{0,64},{4,68},{8,72},{12,76},{16,80},{20,84},{24,88},{28,92},{32,9... | collective-permute-start | bytes 111080 | tf_op jit(solution)/shard_map/ppermute | solution.py:13
  142.5 29.6 %collective-permute-start.13 = (f32[2,13,356]{2,1,0:T(8,128)S(1)}, f32[2,13,356]{2,1,0:T(8,128)S(1)}, u32[]{:S(2)}, u32[]{:S(2)}) collective-permute-start(f32[2,13,356]{2,1,0:T(8,128)S(1)} %concatenate.66), channel_id=1, source_target_pairs={{0,68},{4,72},{8,76},{12,80},{16,84},{20,88},{24,92},{28,96},{32,1... | collective-permute-start | bytes 111080 | tf_op jit(solution)/shard_map/ppermute | solution.py:13
  144.5 29.6 %collective-permute-start.14 = (f32[2,13,356]{2,1,0:T(8,128)S(1)}, f32[2,13,356]{2,1,0:T(8,128)S(1)}, u32[]{:S(2)}, u32[]{:S(2)}) collective-permute-start(f32[2,13,356]{2,1,0:T(8,128)S(1)} %concatenate.66), channel_id=1, source_target_pairs={{0,124},{4,128},{8,132},{12,136},{16,140},{20,144},{24,148},{28,15... | collective-permute-start | bytes 111080 | tf_op jit(solution)/shard_map/ppermute | solution.py:13
  158.0 26.4 %collective-permute-start.15 = (f32[2,13,356]{2,1,0:T(8,128)S(1)}, f32[2,13,356]{2,1,0:T(8,128)S(1)}, u32[]{:S(2)}, u32[]{:S(2)}) collective-permute-start(f32[2,13,356]{2,1,0:T(8,128)S(1)} %concatenate.66), channel_id=1, source_target_pairs={{0,388},{4,392},{8,396},{12,400},{16,404},{20,408},{24,412},{28,41... | collective-permute-start | bytes 111080 | tf_op jit(solution)/shard_map/ppermute | solution.py:13
  160.0 24.4 %collective-permute-start.16 = (f32[2,13,356]{2,1,0:T(8,128)S(1)}, f32[2,13,356]{2,1,0:T(8,128)S(1)}, u32[]{:S(2)}, u32[]{:S(2)}) collective-permute-start(f32[2,13,356]{2,1,0:T(8,128)S(1)} %concatenate.66), channel_id=1, source_target_pairs={{0,444},{4,448},{8,452},{12,456},{16,460},{20,464},{24,468},{28,47... | collective-permute-start | bytes 111080 | tf_op jit(solution)/shard_map/ppermute | solution.py:13
  168.4 16.0 %collective-permute-start.17 = (f32[2,13,356]{2,1,0:T(8,128)S(1)}, f32[2,13,356]{2,1,0:T(8,128)S(1)}, u32[]{:S(2)}, u32[]{:S(2)}) collective-permute-start(f32[2,13,356]{2,1,0:T(8,128)S(1)} %concatenate.66), channel_id=1, source_target_pairs={{0,448},{4,452},{8,456},{12,460},{16,464},{20,468},{24,472},{28,47... | collective-permute-start | bytes 111080 | tf_op jit(solution)/shard_map/ppermute | solution.py:13
  172.1 12.3 %collective-permute-start.18 = (f32[2,13,356]{2,1,0:T(8,128)S(1)}, f32[2,13,356]{2,1,0:T(8,128)S(1)}, u32[]{:S(2)}, u32[]{:S(2)}) collective-permute-start(f32[2,13,356]{2,1,0:T(8,128)S(1)} %concatenate.66), channel_id=1, source_target_pairs={{0,452},{4,456},{8,460},{12,464},{16,468},{20,472},{24,476},{28,48... | collective-permute-start | bytes 111080 | tf_op jit(solution)/shard_map/ppermute | solution.py:13
  174.1 11.4 %collective-permute-start.19 = (f32[2,13,356]{2,1,0:T(8,128)S(1)}, f32[2,13,356]{2,1,0:T(8,128)S(1)}, u32[]{:S(2)}, u32[]{:S(2)}) collective-permute-start(f32[2,13,356]{2,1,0:T(8,128)S(1)} %concatenate.66), channel_id=1, source_target_pairs={{0,508},{4,0},{8,4},{12,8},{16,12},{20,16},{24,20},{28,24},{32,28}... | collective-permute-start | bytes 111080 | tf_op jit(solution)/shard_map/ppermute | solution.py:13
